TPU v7x, 32 devices: a whole 2x2x4 slice. The times are simulated.
32 devices in a mesh: grp: 2 (over x), section: 16 (over z, y, core).
Axes of the slice: x: 2, y: 2, z: 4, core: 2. Of those that a mesh axis runs over, the one named last changes fastest.
Arguments:
- latent: bfloat16 [1536, 64], P(('grp', 'section')), parts along dimension 0, may hold values from -6 to 6
- control_latent: bfloat16 [1536, 64], P(('grp', 'section')), parts along dimension 0, may hold values from -6 to 6
- patch_tiles: int32 [4], replicated, may hold values from 1 to 2, 6 in all
- tile_lists: int32 [2, 6, 3], replicated, may hold values from 0 to 5, as said below
- tile_counts: int32 [2, 6], replicated, may hold values from 1 to 3, as said below
- embed_weight: bfloat16 [64, 3072], replicated, may hold values from -0.75 to 0.75
- control_embed: bfloat16 [64, 3072], replicated, may hold values from -0.75 to 0.75
- modulation: float32 [2, 3, 3072], replicated, may hold values from -4 to 4
- qk_gain: float32 [2, 2, 128], replicated, may hold values from 0.1 to 1.9
- qkv_weight: bfloat16 [16, 3072, 1152], P('section'), may hold values from -0.109375 to 0.109375
- out_weight: bfloat16 [16, 384, 3072], P('section'), may hold values from -0.109375 to 0.109375
- stale_cache: bfloat16 [16, 1536, 768], P('section', 'grp'), parts along dimension 1, may hold values from -6 to 6
- control_gain: float32 [1, 3072], replicated, may hold values from -3 to 3
- final_mod: float32 [2, 3072], replicated, may hold values from -3 to 3
- final_weight: bfloat16 [3072, 64], replicated, may hold values from -0.109375 to 0.109375
Outputs:
- denoised: float32 [1536, 64], P(('grp', 'section')), parts along dimension 0
There are 2 independent parts, one for each index of `grp`. A program takes and returns all parts, laid end to end along the dimension named above; an argument that names none is the same for every part. Nothing has to cross between parts.
Inputs may be any that keep to these rules, and one draw needn't show every extreme that they name: `patch_tiles`: the patches are contiguous and in order and together cover all 6 tiles; the largest has exactly 2 tiles. Entry 0 of tile_lists[b, t] is t itself; the 3 entries of one row are distinct. `tile_counts`: in every block slot some query tile uses all 3 listed tiles.
All inputs are finite; a program needn't handle non-finite values.
Results may differ from a plain program's by a relative error of at most 0.014.
Values may be sent and summed in bfloat16 or wider, within the bound.
No kernel may reach another device: no remote copies, remote signals or barrier semaphores. Data moves between devices by JAX's collectives and lax.ppermute only.
A program may use at most 64 MiB of HBM per device.

v0:
```python
import math
import jax
import jax.numpy as jnp
from jax import lax
from jax.sharding import PartitionSpec as P

D = 3072
HD = 128
HG = 8
C_OUT = 64
TILE = 128
KSEL = 3
PATCHES = 4
TILES = 6
PMAX = 2
EPSILON = 1e-06


def from_partner(value, axis, distance):
    return lax.ppermute(value, axis, [(i, i ^ 1 << distance) for i in range(lax.axis_size(axis))])


def from_behind(value, axis, steps):
    count = lax.axis_size(axis)
    leading, last = (max(0, -steps), min(count, count - steps))
    return lax.ppermute(value, axis, [(source, source + steps) for source in range(leading, last)])


def modulated(hidden, shift_row, scale_row):
    values = hidden.astype(jnp.float32)
    centered = values - jnp.mean(values, axis=-1, keepdims=True)
    variance = jnp.mean(centered * centered, axis=-1, keepdims=True)
    normed = centered * lax.rsqrt(variance + EPSILON)
    return (normed * (1.0 + scale_row) + shift_row).astype(jnp.bfloat16)


def rms_scaled(values, gain_row):
    return (
        values * lax.rsqrt(jnp.mean(values * values, axis=-1, keepdims=True) + EPSILON) * gain_row
    )


def attend_group(
    modded, w_qkv, w_out, memory, gain_pair, start_tile, patch_length, tile_list, tile_limit
):
    row_count = modded.shape[0]
    query_tiles_count = row_count // TILE
    head_count = w_out.shape[0] // HD
    projected = jnp.dot(modded, w_qkv, preferred_element_type=jnp.float32).reshape(
        row_count, 3, head_count, HD
    )
    queries = rms_scaled(projected[:, 0], gain_pair[0]).astype(jnp.bfloat16)
    keys_new = rms_scaled(projected[:, 1], gain_pair[1]).astype(jnp.bfloat16)
    values_new = projected[:, 2].astype(jnp.bfloat16)
    fresh_rows = jnp.concatenate(
        [
            keys_new.reshape(row_count, head_count * HD),
            values_new.reshape(row_count, head_count * HD),
        ],
        axis=1,
    )
    row_start = start_tile * TILE
    previous = lax.dynamic_slice_in_dim(memory, row_start, row_count, 0)
    live_rows = jnp.arange(row_count) < patch_length * TILE
    memory = lax.dynamic_update_slice_in_dim(
        memory, jnp.where(live_rows[:, None], fresh_rows, previous), row_start, 0
    )
    tiled_memory = memory.reshape(-1, TILE, 2, head_count, HD)
    query_tiles = jnp.minimum(start_tile + jnp.arange(query_tiles_count), TILES - 1)
    picked = tile_list[query_tiles]
    used_counts = tile_limit[query_tiles]
    chosen = tiled_memory[picked]
    key_rows = chosen[:, :, :, 0].reshape(query_tiles_count, KSEL * TILE, head_count, HD)
    value_rows = chosen[:, :, :, 1].reshape(query_tiles_count, KSEL * TILE, head_count, HD)
    query_rows = queries.reshape(query_tiles_count, TILE, head_count, HD)
    scores = jnp.einsum(
        "tqhd,tkhd->thqk", query_rows, key_rows, preferred_element_type=jnp.float32
    ) / math.sqrt(HD)
    allowed = (jnp.arange(KSEL * TILE) // TILE)[None, :] < used_counts[:, None]
    scores = jnp.where(allowed[:, None, None, :], scores, -1e30)
    highest = jnp.max(scores, axis=-1, keepdims=True)
    weights = jnp.exp(scores - highest)
    probabilities = (weights / jnp.sum(weights, axis=-1, keepdims=True)).astype(jnp.bfloat16)
    attended = jnp.einsum(
        "thqk,tkhd->tqhd", probabilities, value_rows, preferred_element_type=jnp.float32
    ).astype(jnp.bfloat16)
    attended = attended.reshape(row_count, head_count * HD)
    partial_value = jnp.dot(attended, w_out, preferred_element_type=jnp.float32)
    return (partial_value, memory)


def split_rows(current, upper_half):
    middle = current.shape[0] // 2
    kept = jnp.where(upper_half, current[middle:], current[:middle])
    given = jnp.where(upper_half, current[:middle], current[middle:])
    return (kept, given)


def on_device(
    latent,
    control_latent,
    patch_tiles,
    tile_lists,
    tile_counts,
    embed_weight,
    control_embed,
    modulation,
    qk_gain,
    qkv_weight,
    out_weight,
    stale_cache,
    control_gain,
    final_mod,
    final_weight,
):
    slot_count = lax.axis_size("section") // HG
    control_count = slot_count // 2
    device_index = lax.axis_index("section")
    slot_index = device_index // HG
    group_index = device_index % HG
    is_control = slot_index % 2 == 0
    chain_index = slot_index // 2
    row_count = PMAX * TILE
    share_rows = row_count // HG
    bit_count = HG.bit_length() - 1
    bit_order = list(range(bit_count - 1, -1, -1))
    share_start = jnp.zeros((), jnp.int32)
    for position, bit_index in enumerate(bit_order):
        share_start = share_start + (group_index >> bit_index & 1) * (row_count >> position + 1)
    whole_latent, whole_control = (
        lax.all_gather(latent, "section", axis=0, tiled=True),
        lax.all_gather(control_latent, "section", axis=0, tiled=True),
    )
    padding = ((0, row_count), (0, 0))
    latent_pad = jnp.pad(whole_latent, padding)
    control_pad = jnp.pad(whole_control, padding)
    seq_rows = whole_latent.shape[0]
    memory_start = jnp.pad(stale_cache[0], padding)
    w_qkv = qkv_weight[0]
    w_out = out_weight[0]
    shifts = modulation[slot_index]
    gain_pair = qk_gain[slot_index]
    tile_list = tile_lists[slot_index]
    tile_limit = tile_counts[slot_index]
    control_row = control_gain[jnp.minimum(chain_index, control_count - 1)]
    is_last_main = slot_index == slot_count - 1
    starts = jnp.cumsum(patch_tiles) - patch_tiles

    def reduce_share(partial_value):
        upper_half = group_index >> bit_order[0] & 1 == 1
        kept, given = split_rows(partial_value.astype(jnp.bfloat16), upper_half)
        summed = kept.astype(jnp.float32) + from_partner(given, "section", bit_order[0]).astype(
            jnp.float32
        )
        for bit_index in bit_order[1:]:
            upper_half = group_index >> bit_index & 1 == 1
            kept, given = split_rows(summed, upper_half)
            summed = kept + from_partner(given.astype(jnp.bfloat16), "section", bit_index).astype(
                given.dtype
            )
        return summed

    def gather_rows(gathered):
        for bit_index in reversed(bit_order):
            partner = from_partner(gathered, "section", bit_index)
            upper_half = group_index >> bit_index & 1 == 1
            gathered = jnp.where(
                upper_half,
                jnp.concatenate([partner, gathered]),
                jnp.concatenate([gathered, partner]),
            )
        return gathered

    def run_tick(tick_index, carry):
        inflow_hidden, inflow_control, memory, denoised = carry
        patch_index = tick_index - slot_index
        active = (patch_index >= 0) & (patch_index < PATCHES)
        patch_index = jnp.clip(patch_index, 0, PATCHES - 1)
        start_tile = starts[patch_index]
        patch_length = patch_tiles[patch_index]
        row_start = start_tile * TILE + share_start
        own_latent = lax.dynamic_slice_in_dim(latent_pad, row_start, share_rows, 0)
        own_control = lax.dynamic_slice_in_dim(control_pad, row_start, share_rows, 0)
        embedded = jnp.dot(own_latent, embed_weight, preferred_element_type=jnp.float32)
        conditioned = embedded + jnp.dot(
            own_control, control_embed, preferred_element_type=jnp.float32
        )
        first_slot = slot_index == 0
        current_hidden = jnp.where(first_slot, embedded.astype(jnp.bfloat16), inflow_hidden)
        current_control = jnp.where(first_slot, conditioned.astype(jnp.bfloat16), inflow_control)
        stream = jnp.where(is_control, current_control, current_hidden)
        gathered = gather_rows(stream)

        def compute(memory_in):
            modded = modulated(gathered, shifts[0], shifts[1])
            return attend_group(
                modded,
                w_qkv,
                w_out,
                memory_in,
                gain_pair,
                start_tile,
                patch_length,
                tile_list,
                tile_limit,
            )

        def skipped(memory_in):
            return (jnp.zeros((row_count, w_out.shape[1]), jnp.float32), memory_in)

        partial_value, memory = lax.cond(active, compute, skipped, memory)
        summed = reduce_share(partial_value)
        updated = stream.astype(jnp.float32) + shifts[2] * summed
        new_control = updated.astype(jnp.bfloat16)
        new_hidden = (updated + control_row * current_control.astype(jnp.float32)).astype(
            jnp.bfloat16
        )
        out_hidden = jnp.where(is_control, current_hidden, new_hidden)
        out_control = jnp.where(is_control, new_control, current_control)
        final_rows = jnp.dot(
            modulated(out_hidden, final_mod[0], final_mod[1]),
            final_weight,
            preferred_element_type=jnp.float32,
        )
        live_rows = (
            active & is_last_main & (share_start + jnp.arange(share_rows) < patch_length * TILE)
        )
        previous = lax.dynamic_slice_in_dim(denoised, row_start, share_rows, 0)
        denoised = lax.dynamic_update_slice_in_dim(
            denoised, jnp.where(live_rows[:, None], final_rows, previous), row_start, 0
        )
        inflow_hidden, inflow_control = from_behind((out_hidden, out_control), "section", HG)
        return (inflow_hidden, inflow_control, memory, denoised)

    empty_share = jnp.zeros((share_rows, D), jnp.bfloat16)
    initial = (
        empty_share,
        empty_share,
        memory_start,
        jnp.zeros((seq_rows + row_count, C_OUT), jnp.float32),
    )
    finished = lax.fori_loop(0, slot_count + PATCHES - 1, run_tick, initial)
    return lax.psum_scatter(finished[3][:seq_rows], "section", scatter_dimension=0, tiled=True)


def solution(mesh):
    return jax.shard_map(
        on_device,
        mesh=mesh,
        in_specs=(
            P(("grp", "section"), None),
            P(("grp", "section"), None),
            P(),
            P(),
            P(),
            P(),
            P(),
            P(),
            P(),
            P("section", None, None),
            P("section", None, None),
            P("section", "grp", None),
            P(),
            P(),
            P(),
        ),
        out_specs=P(("grp", "section"), None),
        check_vma=False,
    )
```

profile of v0, /device:TPU:0, one launch (start us, length us, event | category | flops | bytes accessed | tf_op | source)
XLA Modules:
  0.0 692.2 jit_solution(14145736935525604301)
XLA Ops:
  8.5 23.6 %all_gather.6 = bf16[768,64]{1,0:T(8,128)(2,1)S(1)} all-gather(bf16[48,64]{1,0:T(8,128)(2,1)S(1)} %copy-done.7), channel_id=1, replica_groups=mesh['grp'=2,'section'=16] {'section'}, dimensions={0}, use_global_device_ids=true | all-gather | bytes 104448 | tf_op jit(solution)/shard_map/all_gather | solution.py:131
  32.1 17.9 %all_gather.7 = bf16[768,64]{1,0:T(8,128)(2,1)S(1)} all-gather(bf16[48,64]{1,0:T(8,128)(2,1)S(1)} %copy-done.8), channel_id=1, replica_groups=mesh['grp'=2,'section'=16] {'section'}, dimensions={0}, use_global_device_ids=true | all-gather | bytes 104448 | tf_op jit(solution)/shard_map/all_gather | solution.py:132
  54.7 562.6 %while.25 = (s32[]{:T(128)}, bf16[32,3072]{1,0:T(8,128)(2,1)}, bf16[32,3072]{1,0:T(8,128)(2,1)S(1)}, bf16[1024,768]{0,1:T(8,128)(2,1)}, f32[1024,64]{1,0:T(8,128...) while((s32[]{:T(128)}, bf16[32,3072]{1,0:T(8,128)(2,1)}, ...), condition=%wide.region_12.13_spmd, body=%wide.region_1.12_spmd.sunk | while | flops 2714486016 | bytes 100601624 | solution.py:242
  62.3 9.7 %collective-permute-done.1 = bf16[64,3072]{1,0:T(8,128)(2,1)S(1)} collective-permute-done((bf16[64,3072]{1,0:T(8,128)(2,1)S(1)}, bf16[64,3072]{1,0:T(8,128)(2,1)S(1)}, u32[]{:S(2)}, u32[]{:S(2)}) %collective-permute-start.1) | collective-permute-done | bytes 393248 | tf_op jit(solution)/shard_map/while/body/eval_jaxpr/ppermute | solution.py:20
  73.1 18.2 %collective-permute-done.2 = bf16[128,3072]{1,0:T(8,128)(2,1)} collective-permute-done((bf16[128,3072]{1,0:T(8,128)(2,1)S(1)}, bf16[128,3072]{1,0:T(8,128)(2,1)}, u32[]{:S(2)}, u32[]{:S(2)}) %collective-permute-start.2) | collective-permute-done | bytes 786464 | tf_op jit(solution)/shard_map/while/body/eval_jaxpr/ppermute | solution.py:20
  93.3 25.1 %conditional.2 = (bf16[1024,768]{0,1:T(8,128)(2,1)}, bf16[128,3072]{1,0:T(8,128)(2,1)S(1)}, bf16[128,3072]{1,0:T(8,128)(2,1)S(1)}) conditional(s32[]{:T(128)} %convert_element_type.288, bf16[1024,768]{0,1:T(8,128)(2,1)} %get-tuple-element.1047, (s32[]{:T(128)}, pred[]{:T(512)}, bf16[256,3072]{1,0:T(8,128)(2,1)S(1)}, bf16[256,3072]{1,0:T(8,128)(2,1)S(1)}, ...), branch_computations={%region_2.2_spmd, %region_3.9_spmd} | conditional | flops 2658447616 | bytes 57946768 | solution.py:211
  118.9 17.8 %collective-permute-done.3 = bf16[128,3072]{1,0:T(8,128)(2,1)S(1)} collective-permute-done((bf16[128,3072]{1,0:T(8,128)(2,1)S(1)}, bf16[128,3072]{1,0:T(8,128)(2,1)S(1)}, u32[]{:S(2)}, u32[]{:S(2)}) %collective-permute-start.3) | collective-permute-done | bytes 786464 | tf_op jit(solution)/shard_map/while/body/eval_jaxpr/ppermute | solution.py:20
  165.9 9.5 %collective-permute-done.1 = bf16[64,3072]{1,0:T(8,128)(2,1)S(1)} collective-permute-done((bf16[64,3072]{1,0:T(8,128)(2,1)S(1)}, bf16[64,3072]{1,0:T(8,128)(2,1)S(1)}, u32[]{:S(2)}, u32[]{:S(2)}) %collective-permute-start.1) | collective-permute-done | bytes 393248 | tf_op jit(solution)/shard_map/while/body/eval_jaxpr/ppermute | solution.py:20
  175.5 9.3 %collective-permute-start.2 = (bf16[128,3072]{1,0:T(8,128)(2,1)S(1)}, bf16[128,3072]{1,0:T(8,128)(2,1)}, u32[]{:S(2)}, u32[]{:S(2)}) collective-permute-start(bf16[128,3072]{1,0:T(8,128)(2,1)S(1)} %maximum_select_fusion.6), channel_id=1, source_target_pairs={{0,4},{1,5},{2,6},{3,7},{4,0},{5,1},{6,2},{7,3},{8,12},{9,13},{10,... | collective-permute-start | bytes 2359304 | tf_op jit(solution)/shard_map/while/body/eval_jaxpr/ppermute | solution.py:20
  185.4 16.4 %collective-permute-done.2 = bf16[128,3072]{1,0:T(8,128)(2,1)} collective-permute-done((bf16[128,3072]{1,0:T(8,128)(2,1)S(1)}, bf16[128,3072]{1,0:T(8,128)(2,1)}, u32[]{:S(2)}, u32[]{:S(2)}) %collective-permute-start.2) | collective-permute-done | bytes 786464 | tf_op jit(solution)/shard_map/while/body/eval_jaxpr/ppermute | solution.py:20
  203.9 25.1 %conditional.2 = (bf16[1024,768]{0,1:T(8,128)(2,1)}, bf16[128,3072]{1,0:T(8,128)(2,1)S(1)}, bf16[128,3072]{1,0:T(8,128)(2,1)S(1)}) conditional(s32[]{:T(128)} %convert_element_type.288, bf16[1024,768]{0,1:T(8,128)(2,1)} %get-tuple-element.1047, (s32[]{:T(128)}, pred[]{:T(512)}, bf16[256,3072]{1,0:T(8,128)(2,1)S(1)}, bf16[256,3072]{1,0:T(8,128)(2,1)S(1)}, ...), branch_computations={%region_2.2_spmd, %region_3.9_spmd} | conditional | flops 2658447616 | bytes 57946768 | solution.py:211
  231.0 16.4 %collective-permute-done.3 = bf16[128,3072]{1,0:T(8,128)(2,1)S(1)} collective-permute-done((bf16[128,3072]{1,0:T(8,128)(2,1)S(1)}, bf16[128,3072]{1,0:T(8,128)(2,1)S(1)}, u32[]{:S(2)}, u32[]{:S(2)}) %collective-permute-start.3) | collective-permute-done | bytes 786464 | tf_op jit(solution)/shard_map/while/body/eval_jaxpr/ppermute | solution.py:20
  249.5 7.2 %collective-permute-done.4 = bf16[64,3072]{1,0:T(8,128)(2,1)S(1)} collective-permute-done((bf16[64,3072]{1,0:T(8,128)(2,1)S(1)}, bf16[64,3072]{1,0:T(8,128)(2,1)S(1)}, u32[]{:S(2)}, u32[]{:S(2)}) %collective-permute-start.4) | collective-permute-done | bytes 393248 | tf_op jit(solution)/shard_map/while/body/eval_jaxpr/ppermute | solution.py:20
  280.4 9.5 %collective-permute-done.1 = bf16[64,3072]{1,0:T(8,128)(2,1)S(1)} collective-permute-done((bf16[64,3072]{1,0:T(8,128)(2,1)S(1)}, bf16[64,3072]{1,0:T(8,128)(2,1)S(1)}, u32[]{:S(2)}, u32[]{:S(2)}) %collective-permute-start.1) | collective-permute-done | bytes 393248 | tf_op jit(solution)/shard_map/while/body/eval_jaxpr/ppermute | solution.py:20
  290.0 9.6 %collective-permute-start.2 = (bf16[128,3072]{1,0:T(8,128)(2,1)S(1)}, bf16[128,3072]{1,0:T(8,128)(2,1)}, u32[]{:S(2)}, u32[]{:S(2)}) collective-permute-start(bf16[128,3072]{1,0:T(8,128)(2,1)S(1)} %maximum_select_fusion.6), channel_id=1, source_target_pairs={{0,4},{1,5},{2,6},{3,7},{4,0},{5,1},{6,2},{7,3},{8,12},{9,13},{10,... | collective-permute-start | bytes 2359304 | tf_op jit(solution)/shard_map/while/body/eval_jaxpr/ppermute | solution.py:20
  300.3 16.4 %collective-permute-done.2 = bf16[128,3072]{1,0:T(8,128)(2,1)} collective-permute-done((bf16[128,3072]{1,0:T(8,128)(2,1)S(1)}, bf16[128,3072]{1,0:T(8,128)(2,1)}, u32[]{:S(2)}, u32[]{:S(2)}) %collective-permute-start.2) | collective-permute-done | bytes 786464 | tf_op jit(solution)/shard_map/while/body/eval_jaxpr/ppermute | solution.py:20
  318.8 25.1 %conditional.2 = (bf16[1024,768]{0,1:T(8,128)(2,1)}, bf16[128,3072]{1,0:T(8,128)(2,1)S(1)}, bf16[128,3072]{1,0:T(8,128)(2,1)S(1)}) conditional(s32[]{:T(128)} %convert_element_type.288, bf16[1024,768]{0,1:T(8,128)(2,1)} %get-tuple-element.1047, (s32[]{:T(128)}, pred[]{:T(512)}, bf16[256,3072]{1,0:T(8,128)(2,1)S(1)}, bf16[256,3072]{1,0:T(8,128)(2,1)S(1)}, ...), branch_computations={%region_2.2_spmd, %region_3.9_spmd} | conditional | flops 2658447616 | bytes 57946768 | solution.py:211
  345.8 16.4 %collective-permute-done.3 = bf16[128,3072]{1,0:T(8,128)(2,1)S(1)} collective-permute-done((bf16[128,3072]{1,0:T(8,128)(2,1)S(1)}, bf16[128,3072]{1,0:T(8,128)(2,1)S(1)}, u32[]{:S(2)}, u32[]{:S(2)}) %collective-permute-start.3) | collective-permute-done | bytes 786464 | tf_op jit(solution)/shard_map/while/body/eval_jaxpr/ppermute | solution.py:20
  364.4 7.2 %collective-permute-done.4 = bf16[64,3072]{1,0:T(8,128)(2,1)S(1)} collective-permute-done((bf16[64,3072]{1,0:T(8,128)(2,1)S(1)}, bf16[64,3072]{1,0:T(8,128)(2,1)S(1)}, u32[]{:S(2)}, u32[]{:S(2)}) %collective-permute-start.4) | collective-permute-done | bytes 393248 | tf_op jit(solution)/shard_map/while/body/eval_jaxpr/ppermute | solution.py:20
  395.2 9.5 %collective-permute-done.1 = bf16[64,3072]{1,0:T(8,128)(2,1)S(1)} collective-permute-done((bf16[64,3072]{1,0:T(8,128)(2,1)S(1)}, bf16[64,3072]{1,0:T(8,128)(2,1)S(1)}, u32[]{:S(2)}, u32[]{:S(2)}) %collective-permute-start.1) | collective-permute-done | bytes 393248 | tf_op jit(solution)/shard_map/while/body/eval_jaxpr/ppermute | solution.py:20
  404.9 9.6 %collective-permute-start.2 = (bf16[128,3072]{1,0:T(8,128)(2,1)S(1)}, bf16[128,3072]{1,0:T(8,128)(2,1)}, u32[]{:S(2)}, u32[]{:S(2)}) collective-permute-start(bf16[128,3072]{1,0:T(8,128)(2,1)S(1)} %maximum_select_fusion.6), channel_id=1, source_target_pairs={{0,4},{1,5},{2,6},{3,7},{4,0},{5,1},{6,2},{7,3},{8,12},{9,13},{10,... | collective-permute-start | bytes 2359304 | tf_op jit(solution)/shard_map/while/body/eval_jaxpr/ppermute | solution.py:20
  415.1 16.4 %collective-permute-done.2 = bf16[128,3072]{1,0:T(8,128)(2,1)} collective-permute-done((bf16[128,3072]{1,0:T(8,128)(2,1)S(1)}, bf16[128,3072]{1,0:T(8,128)(2,1)}, u32[]{:S(2)}, u32[]{:S(2)}) %collective-permute-start.2) | collective-permute-done | bytes 786464 | tf_op jit(solution)/shard_map/while/body/eval_jaxpr/ppermute | solution.py:20
  433.6 25.2 %conditional.2 = (bf16[1024,768]{0,1:T(8,128)(2,1)}, bf16[128,3072]{1,0:T(8,128)(2,1)S(1)}, bf16[128,3072]{1,0:T(8,128)(2,1)S(1)}) conditional(s32[]{:T(128)} %convert_element_type.288, bf16[1024,768]{0,1:T(8,128)(2,1)} %get-tuple-element.1047, (s32[]{:T(128)}, pred[]{:T(512)}, bf16[256,3072]{1,0:T(8,128)(2,1)S(1)}, bf16[256,3072]{1,0:T(8,128)(2,1)S(1)}, ...), branch_computations={%region_2.2_spmd, %region_3.9_spmd} | conditional | flops 2658447616 | bytes 57946768 | solution.py:211
  460.7 16.4 %collective-permute-done.3 = bf16[128,3072]{1,0:T(8,128)(2,1)S(1)} collective-permute-done((bf16[128,3072]{1,0:T(8,128)(2,1)S(1)}, bf16[128,3072]{1,0:T(8,128)(2,1)S(1)}, u32[]{:S(2)}, u32[]{:S(2)}) %collective-permute-start.3) | collective-permute-done | bytes 786464 | tf_op jit(solution)/shard_map/while/body/eval_jaxpr/ppermute | solution.py:20
  479.3 7.2 %collective-permute-done.4 = bf16[64,3072]{1,0:T(8,128)(2,1)S(1)} collective-permute-done((bf16[64,3072]{1,0:T(8,128)(2,1)S(1)}, bf16[64,3072]{1,0:T(8,128)(2,1)S(1)}, u32[]{:S(2)}, u32[]{:S(2)}) %collective-permute-start.4) | collective-permute-done | bytes 393248 | tf_op jit(solution)/shard_map/while/body/eval_jaxpr/ppermute | solution.py:20
  510.1 9.5 %collective-permute-done.1 = bf16[64,3072]{1,0:T(8,128)(2,1)S(1)} collective-permute-done((bf16[64,3072]{1,0:T(8,128)(2,1)S(1)}, bf16[64,3072]{1,0:T(8,128)(2,1)S(1)}, u32[]{:S(2)}, u32[]{:S(2)}) %collective-permute-start.1) | collective-permute-done | bytes 393248 | tf_op jit(solution)/shard_map/while/body/eval_jaxpr/ppermute | solution.py:20
  519.7 9.6 %collective-permute-start.2 = (bf16[128,3072]{1,0:T(8,128)(2,1)S(1)}, bf16[128,3072]{1,0:T(8,128)(2,1)}, u32[]{:S(2)}, u32[]{:S(2)}) collective-permute-start(bf16[128,3072]{1,0:T(8,128)(2,1)S(1)} %maximum_select_fusion.6), channel_id=1, source_target_pairs={{0,4},{1,5},{2,6},{3,7},{4,0},{5,1},{6,2},{7,3},{8,12},{9,13},{10,... | collective-permute-start | bytes 2359304 | tf_op jit(solution)/shard_map/while/body/eval_jaxpr/ppermute | solution.py:20
  530.0 16.4 %collective-permute-done.2 = bf16[128,3072]{1,0:T(8,128)(2,1)} collective-permute-done((bf16[128,3072]{1,0:T(8,128)(2,1)S(1)}, bf16[128,3072]{1,0:T(8,128)(2,1)}, u32[]{:S(2)}, u32[]{:S(2)}) %collective-permute-start.2) | collective-permute-done | bytes 786464 | tf_op jit(solution)/shard_map/while/body/eval_jaxpr/ppermute | solution.py:20
  550.6 16.4 %collective-permute-done.3 = bf16[128,3072]{1,0:T(8,128)(2,1)S(1)} collective-permute-done((bf16[128,3072]{1,0:T(8,128)(2,1)S(1)}, bf16[128,3072]{1,0:T(8,128)(2,1)S(1)}, u32[]{:S(2)}, u32[]{:S(2)}) %collective-permute-start.3) | collective-permute-done | bytes 786464 | tf_op jit(solution)/shard_map/while/body/eval_jaxpr/ppermute | solution.py:20
  569.1 7.2 %collective-permute-done.4 = bf16[64,3072]{1,0:T(8,128)(2,1)S(1)} collective-permute-done((bf16[64,3072]{1,0:T(8,128)(2,1)S(1)}, bf16[64,3072]{1,0:T(8,128)(2,1)S(1)}, u32[]{:S(2)}, u32[]{:S(2)}) %collective-permute-start.4) | collective-permute-done | bytes 393248 | tf_op jit(solution)/shard_map/while/body/eval_jaxpr/ppermute | solution.py:20
  578.3 31.0 %collective-permute-start.6 = (bf16[32,3072]{1,0:T(8,128)(2,1)S(1)}, bf16[32,3072]{1,0:T(8,128)(2,1)}, u32[]{:S(2)}, u32[]{:S(2)}) collective-permute-start(bf16[32,3072]{1,0:T(8,128)(2,1)S(1)} %get-tuple-element.999), channel_id=1, source_target_pairs={{0,8},{1,9},{2,10},{3,11},{4,12},{5,13},{6,14},{7,15},{16,24},{17,... | collective-permute-start | bytes 589832 | tf_op jit(solution)/shard_map/while/body/eval_jaxpr/ppermute | solution.py:26
  619.1 66.3 %reduce-scatter.2.cloned.1.call-done = f32[48,64]{1,0:T(8,128)} async-done(((f32[768,64]{1,0:T(8,128)}), f32[48,64]{1,0:T(8,128)}) %reduce-scatter.2.cloned.1.call-update) | async-done | bytes 12304 | tf_op jit(solution)/shard_map/reduce_scatter | solution.py:243
  (394 shorter events, 245.0 us)
Async XLA Ops:
  6.6 678.8 %reduce-scatter.2.cloned.1.call-start = ((), (), s32[]{:S(2)}) async-start(), calls=%async_computation.1 | async-start | bytes 417792 | tf_op jit(solution)/shard_map/reduce_scatter | solution.py:243
  60.6 11.4 %collective-permute-start.1 = (bf16[64,3072]{1,0:T(8,128)(2,1)S(1)}, bf16[64,3072]{1,0:T(8,128)(2,1)S(1)}, u32[]{:S(2)}, u32[]{:S(2)}) collective-permute-start(bf16[64,3072]{1,0:T(8,128)(2,1)S(1)} %maximum_select_fusion.5), channel_id=1, source_target_pairs={{0,2},{1,3},{2,0},{3,1},{4,6},{5,7},{6,4},{7,5},{8,10},{9,11},{10,... | collective-permute-start | bytes 1179656 | tf_op jit(solution)/shard_map/while/body/eval_jaxpr/ppermute | solution.py:20
  72.2 19.1 %collective-permute-start.2 = (bf16[128,3072]{1,0:T(8,128)(2,1)S(1)}, bf16[128,3072]{1,0:T(8,128)(2,1)}, u32[]{:S(2)}, u32[]{:S(2)}) collective-permute-start(bf16[128,3072]{1,0:T(8,128)(2,1)S(1)} %maximum_select_fusion.6), channel_id=1, source_target_pairs={{0,4},{1,5},{2,6},{3,7},{4,0},{5,1},{6,2},{7,3},{8,12},{9,13},{10,... | collective-permute-start | bytes 2359304 | tf_op jit(solution)/shard_map/while/body/eval_jaxpr/ppermute | solution.py:20
  118.6 18.1 %collective-permute-start.3 = (bf16[128,3072]{1,0:T(8,128)(2,1)S(1)}, bf16[128,3072]{1,0:T(8,128)(2,1)S(1)}, u32[]{:S(2)}, u32[]{:S(2)}) collective-permute-start(bf16[128,3072]{1,0:T(8,128)(2,1)S(1)} %broadcast_select_fusion.7), channel_id=1, source_target_pairs={{0,4},{1,5},{2,6},{3,7},{4,0},{5,1},{6,2},{7,3},{8,12},{9,13},{10,... | collective-permute-start | bytes 2359304 | tf_op jit(solution)/shard_map/while/body/eval_jaxpr/ppermute | solution.py:20
  137.1 8.9 %collective-permute-start.4 = (bf16[64,3072]{1,0:T(8,128)(2,1)S(1)}, bf16[64,3072]{1,0:T(8,128)(2,1)S(1)}, u32[]{:S(2)}, u32[]{:S(2)}) collective-permute-start(bf16[64,3072]{1,0:T(8,128)(2,1)S(1)} %select_convert_fusion.4), channel_id=1, source_target_pairs={{0,2},{1,3},{2,0},{3,1},{4,6},{5,7},{6,4},{7,5},{8,10},{9,11},{10,... | collective-permute-start | bytes 1179656 | tf_op jit(solution)/shard_map/while/body/eval_jaxpr/ppermute | solution.py:20
  147.9 6.6 collective-permute-start.6
  150.0 8.2 %collective-permute-start.7 = (bf16[32,3072]{1,0:T(8,128)(2,1)S(1)}, bf16[32,3072]{1,0:T(8,128)(2,1)S(1)}, u32[]{:S(2)}, u32[]{:S(2)}) collective-permute-start(bf16[32,3072]{1,0:T(8,128)(2,1)S(1)} %convert_select_fusion.4), channel_id=1, source_target_pairs={{0,8},{1,9},{2,10},{3,11},{4,12},{5,13},{6,14},{7,15},{16,24},{17,... | collective-permute-start | bytes 589832 | tf_op jit(solution)/shard_map/while/body/eval_jaxpr/ppermute | solution.py:26
  164.1 11.2 %collective-permute-start.1 = (bf16[64,3072]{1,0:T(8,128)(2,1)S(1)}, bf16[64,3072]{1,0:T(8,128)(2,1)S(1)}, u32[]{:S(2)}, u32[]{:S(2)}) collective-permute-start(bf16[64,3072]{1,0:T(8,128)(2,1)S(1)} %maximum_select_fusion.5), channel_id=1, source_target_pairs={{0,2},{1,3},{2,0},{3,1},{4,6},{5,7},{6,4},{7,5},{8,10},{9,11},{10,... | collective-permute-start | bytes 1179656 | tf_op jit(solution)/shard_map/while/body/eval_jaxpr/ppermute | solution.py:20
  175.5 26.4 %collective-permute-start.2 = (bf16[128,3072]{1,0:T(8,128)(2,1)S(1)}, bf16[128,3072]{1,0:T(8,128)(2,1)}, u32[]{:S(2)}, u32[]{:S(2)}) collective-permute-start(bf16[128,3072]{1,0:T(8,128)(2,1)S(1)} %maximum_select_fusion.6), channel_id=1, source_target_pairs={{0,4},{1,5},{2,6},{3,7},{4,0},{5,1},{6,2},{7,3},{8,12},{9,13},{10,... | collective-permute-start | bytes 2359304 | tf_op jit(solution)/shard_map/while/body/eval_jaxpr/ppermute | solution.py:20
  229.2 18.2 %collective-permute-start.3 = (bf16[128,3072]{1,0:T(8,128)(2,1)S(1)}, bf16[128,3072]{1,0:T(8,128)(2,1)S(1)}, u32[]{:S(2)}, u32[]{:S(2)}) collective-permute-start(bf16[128,3072]{1,0:T(8,128)(2,1)S(1)} %broadcast_select_fusion.7), channel_id=1, source_target_pairs={{0,4},{1,5},{2,6},{3,7},{4,0},{5,1},{6,2},{7,3},{8,12},{9,13},{10,... | collective-permute-start | bytes 2359304 | tf_op jit(solution)/shard_map/while/body/eval_jaxpr/ppermute | solution.py:20
  247.8 8.9 %collective-permute-start.4 = (bf16[64,3072]{1,0:T(8,128)(2,1)S(1)}, bf16[64,3072]{1,0:T(8,128)(2,1)S(1)}, u32[]{:S(2)}, u32[]{:S(2)}) collective-permute-start(bf16[64,3072]{1,0:T(8,128)(2,1)S(1)} %select_convert_fusion.4), channel_id=1, source_target_pairs={{0,2},{1,3},{2,0},{3,1},{4,6},{5,7},{6,4},{7,5},{8,10},{9,11},{10,... | collective-permute-start | bytes 1179656 | tf_op jit(solution)/shard_map/while/body/eval_jaxpr/ppermute | solution.py:20
  258.7 10.7 %collective-permute-start.6 = (bf16[32,3072]{1,0:T(8,128)(2,1)S(1)}, bf16[32,3072]{1,0:T(8,128)(2,1)}, u32[]{:S(2)}, u32[]{:S(2)}) collective-permute-start(bf16[32,3072]{1,0:T(8,128)(2,1)S(1)} %get-tuple-element.999), channel_id=1, source_target_pairs={{0,8},{1,9},{2,10},{3,11},{4,12},{5,13},{6,14},{7,15},{16,24},{17,... | collective-permute-start | bytes 589832 | tf_op jit(solution)/shard_map/while/body/eval_jaxpr/ppermute | solution.py:26
  264.8 7.9 %collective-permute-start.7 = (bf16[32,3072]{1,0:T(8,128)(2,1)S(1)}, bf16[32,3072]{1,0:T(8,128)(2,1)S(1)}, u32[]{:S(2)}, u32[]{:S(2)}) collective-permute-start(bf16[32,3072]{1,0:T(8,128)(2,1)S(1)} %convert_select_fusion.4), channel_id=1, source_target_pairs={{0,8},{1,9},{2,10},{3,11},{4,12},{5,13},{6,14},{7,15},{16,24},{17,... | collective-permute-start | bytes 589832 | tf_op jit(solution)/shard_map/while/body/eval_jaxpr/ppermute | solution.py:26
  278.6 11.2 %collective-permute-start.1 = (bf16[64,3072]{1,0:T(8,128)(2,1)S(1)}, bf16[64,3072]{1,0:T(8,128)(2,1)S(1)}, u32[]{:S(2)}, u32[]{:S(2)}) collective-permute-start(bf16[64,3072]{1,0:T(8,128)(2,1)S(1)} %maximum_select_fusion.5), channel_id=1, source_target_pairs={{0,2},{1,3},{2,0},{3,1},{4,6},{5,7},{6,4},{7,5},{8,10},{9,11},{10,... | collective-permute-start | bytes 1179656 | tf_op jit(solution)/shard_map/while/body/eval_jaxpr/ppermute | solution.py:20
  290.0 26.7 %collective-permute-start.2 = (bf16[128,3072]{1,0:T(8,128)(2,1)S(1)}, bf16[128,3072]{1,0:T(8,128)(2,1)}, u32[]{:S(2)}, u32[]{:S(2)}) collective-permute-start(bf16[128,3072]{1,0:T(8,128)(2,1)S(1)} %maximum_select_fusion.6), channel_id=1, source_target_pairs={{0,4},{1,5},{2,6},{3,7},{4,0},{5,1},{6,2},{7,3},{8,12},{9,13},{10,... | collective-permute-start | bytes 2359304 | tf_op jit(solution)/shard_map/while/body/eval_jaxpr/ppermute | solution.py:20
  344.0 18.2 %collective-permute-start.3 = (bf16[128,3072]{1,0:T(8,128)(2,1)S(1)}, bf16[128,3072]{1,0:T(8,128)(2,1)S(1)}, u32[]{:S(2)}, u32[]{:S(2)}) collective-permute-start(bf16[128,3072]{1,0:T(8,128)(2,1)S(1)} %broadcast_select_fusion.7), channel_id=1, source_target_pairs={{0,4},{1,5},{2,6},{3,7},{4,0},{5,1},{6,2},{7,3},{8,12},{9,13},{10,... | collective-permute-start | bytes 2359304 | tf_op jit(solution)/shard_map/while/body/eval_jaxpr/ppermute | solution.py:20
  362.6 8.9 %collective-permute-start.4 = (bf16[64,3072]{1,0:T(8,128)(2,1)S(1)}, bf16[64,3072]{1,0:T(8,128)(2,1)S(1)}, u32[]{:S(2)}, u32[]{:S(2)}) collective-permute-start(bf16[64,3072]{1,0:T(8,128)(2,1)S(1)} %select_convert_fusion.4), channel_id=1, source_target_pairs={{0,2},{1,3},{2,0},{3,1},{4,6},{5,7},{6,4},{7,5},{8,10},{9,11},{10,... | collective-permute-start | bytes 1179656 | tf_op jit(solution)/shard_map/while/body/eval_jaxpr/ppermute | solution.py:20
  373.5 10.6 %collective-permute-start.6 = (bf16[32,3072]{1,0:T(8,128)(2,1)S(1)}, bf16[32,3072]{1,0:T(8,128)(2,1)}, u32[]{:S(2)}, u32[]{:S(2)}) collective-permute-start(bf16[32,3072]{1,0:T(8,128)(2,1)S(1)} %get-tuple-element.999), channel_id=1, source_target_pairs={{0,8},{1,9},{2,10},{3,11},{4,12},{5,13},{6,14},{7,15},{16,24},{17,... | collective-permute-start | bytes 589832 | tf_op jit(solution)/shard_map/while/body/eval_jaxpr/ppermute | solution.py:26
  379.7 7.9 %collective-permute-start.7 = (bf16[32,3072]{1,0:T(8,128)(2,1)S(1)}, bf16[32,3072]{1,0:T(8,128)(2,1)S(1)}, u32[]{:S(2)}, u32[]{:S(2)}) collective-permute-start(bf16[32,3072]{1,0:T(8,128)(2,1)S(1)} %convert_select_fusion.4), channel_id=1, source_target_pairs={{0,8},{1,9},{2,10},{3,11},{4,12},{5,13},{6,14},{7,15},{16,24},{17,... | collective-permute-start | bytes 589832 | tf_op jit(solution)/shard_map/while/body/eval_jaxpr/ppermute | solution.py:26
  393.5 11.2 %collective-permute-start.1 = (bf16[64,3072]{1,0:T(8,128)(2,1)S(1)}, bf16[64,3072]{1,0:T(8,128)(2,1)S(1)}, u32[]{:S(2)}, u32[]{:S(2)}) collective-permute-start(bf16[64,3072]{1,0:T(8,128)(2,1)S(1)} %maximum_select_fusion.5), channel_id=1, source_target_pairs={{0,2},{1,3},{2,0},{3,1},{4,6},{5,7},{6,4},{7,5},{8,10},{9,11},{10,... | collective-permute-start | bytes 1179656 | tf_op jit(solution)/shard_map/while/body/eval_jaxpr/ppermute | solution.py:20
  404.9 26.7 %collective-permute-start.2 = (bf16[128,3072]{1,0:T(8,128)(2,1)S(1)}, bf16[128,3072]{1,0:T(8,128)(2,1)}, u32[]{:S(2)}, u32[]{:S(2)}) collective-permute-start(bf16[128,3072]{1,0:T(8,128)(2,1)S(1)} %maximum_select_fusion.6), channel_id=1, source_target_pairs={{0,4},{1,5},{2,6},{3,7},{4,0},{5,1},{6,2},{7,3},{8,12},{9,13},{10,... | collective-permute-start | bytes 2359304 | tf_op jit(solution)/shard_map/while/body/eval_jaxpr/ppermute | solution.py:20
  458.9 18.2 %collective-permute-start.3 = (bf16[128,3072]{1,0:T(8,128)(2,1)S(1)}, bf16[128,3072]{1,0:T(8,128)(2,1)S(1)}, u32[]{:S(2)}, u32[]{:S(2)}) collective-permute-start(bf16[128,3072]{1,0:T(8,128)(2,1)S(1)} %broadcast_select_fusion.7), channel_id=1, source_target_pairs={{0,4},{1,5},{2,6},{3,7},{4,0},{5,1},{6,2},{7,3},{8,12},{9,13},{10,... | collective-permute-start | bytes 2359304 | tf_op jit(solution)/shard_map/while/body/eval_jaxpr/ppermute | solution.py:20
  477.5 8.9 %collective-permute-start.4 = (bf16[64,3072]{1,0:T(8,128)(2,1)S(1)}, bf16[64,3072]{1,0:T(8,128)(2,1)S(1)}, u32[]{:S(2)}, u32[]{:S(2)}) collective-permute-start(bf16[64,3072]{1,0:T(8,128)(2,1)S(1)} %select_convert_fusion.4), channel_id=1, source_target_pairs={{0,2},{1,3},{2,0},{3,1},{4,6},{5,7},{6,4},{7,5},{8,10},{9,11},{10,... | collective-permute-start | bytes 1179656 | tf_op jit(solution)/shard_map/while/body/eval_jaxpr/ppermute | solution.py:20
  488.4 10.6 %collective-permute-start.6 = (bf16[32,3072]{1,0:T(8,128)(2,1)S(1)}, bf16[32,3072]{1,0:T(8,128)(2,1)}, u32[]{:S(2)}, u32[]{:S(2)}) collective-permute-start(bf16[32,3072]{1,0:T(8,128)(2,1)S(1)} %get-tuple-element.999), channel_id=1, source_target_pairs={{0,8},{1,9},{2,10},{3,11},{4,12},{5,13},{6,14},{7,15},{16,24},{17,... | collective-permute-start | bytes 589832 | tf_op jit(solution)/shard_map/while/body/eval_jaxpr/ppermute | solution.py:26
  494.5 7.9 %collective-permute-start.7 = (bf16[32,3072]{1,0:T(8,128)(2,1)S(1)}, bf16[32,3072]{1,0:T(8,128)(2,1)S(1)}, u32[]{:S(2)}, u32[]{:S(2)}) collective-permute-start(bf16[32,3072]{1,0:T(8,128)(2,1)S(1)} %convert_select_fusion.4), channel_id=1, source_target_pairs={{0,8},{1,9},{2,10},{3,11},{4,12},{5,13},{6,14},{7,15},{16,24},{17,... | collective-permute-start | bytes 589832 | tf_op jit(solution)/shard_map/while/body/eval_jaxpr/ppermute | solution.py:26
  508.3 11.2 %collective-permute-start.1 = (bf16[64,3072]{1,0:T(8,128)(2,1)S(1)}, bf16[64,3072]{1,0:T(8,128)(2,1)S(1)}, u32[]{:S(2)}, u32[]{:S(2)}) collective-permute-start(bf16[64,3072]{1,0:T(8,128)(2,1)S(1)} %maximum_select_fusion.5), channel_id=1, source_target_pairs={{0,2},{1,3},{2,0},{3,1},{4,6},{5,7},{6,4},{7,5},{8,10},{9,11},{10,... | collective-permute-start | bytes 1179656 | tf_op jit(solution)/shard_map/while/body/eval_jaxpr/ppermute | solution.py:20
  519.7 26.7 %collective-permute-start.2 = (bf16[128,3072]{1,0:T(8,128)(2,1)S(1)}, bf16[128,3072]{1,0:T(8,128)(2,1)}, u32[]{:S(2)}, u32[]{:S(2)}) collective-permute-start(bf16[128,3072]{1,0:T(8,128)(2,1)S(1)} %maximum_select_fusion.6), channel_id=1, source_target_pairs={{0,4},{1,5},{2,6},{3,7},{4,0},{5,1},{6,2},{7,3},{8,12},{9,13},{10,... | collective-permute-start | bytes 2359304 | tf_op jit(solution)/shard_map/while/body/eval_jaxpr/ppermute | solution.py:20
  548.8 18.2 %collective-permute-start.3 = (bf16[128,3072]{1,0:T(8,128)(2,1)S(1)}, bf16[128,3072]{1,0:T(8,128)(2,1)S(1)}, u32[]{:S(2)}, u32[]{:S(2)}) collective-permute-start(bf16[128,3072]{1,0:T(8,128)(2,1)S(1)} %broadcast_select_fusion.7), channel_id=1, source_target_pairs={{0,4},{1,5},{2,6},{3,7},{4,0},{5,1},{6,2},{7,3},{8,12},{9,13},{10,... | collective-permute-start | bytes 2359304 | tf_op jit(solution)/shard_map/while/body/eval_jaxpr/ppermute | solution.py:20
  567.4 8.9 %collective-permute-start.4 = (bf16[64,3072]{1,0:T(8,128)(2,1)S(1)}, bf16[64,3072]{1,0:T(8,128)(2,1)S(1)}, u32[]{:S(2)}, u32[]{:S(2)}) collective-permute-start(bf16[64,3072]{1,0:T(8,128)(2,1)S(1)} %select_convert_fusion.4), channel_id=1, source_target_pairs={{0,2},{1,3},{2,0},{3,1},{4,6},{5,7},{6,4},{7,5},{8,10},{9,11},{10,... | collective-permute-start | bytes 1179656 | tf_op jit(solution)/shard_map/while/body/eval_jaxpr/ppermute | solution.py:20
  576.5 1.5 collective-permute-start.5
  578.3 35.6 %collective-permute-start.6 = (bf16[32,3072]{1,0:T(8,128)(2,1)S(1)}, bf16[32,3072]{1,0:T(8,128)(2,1)}, u32[]{:S(2)}, u32[]{:S(2)}) collective-permute-start(bf16[32,3072]{1,0:T(8,128)(2,1)S(1)} %get-tuple-element.999), channel_id=1, source_target_pairs={{0,8},{1,9},{2,10},{3,11},{4,12},{5,13},{6,14},{7,15},{16,24},{17,... | collective-permute-start | bytes 589832 | tf_op jit(solution)/shard_map/while/body/eval_jaxpr/ppermute | solution.py:26
  609.4 7.9 %collective-permute-start.7 = (bf16[32,3072]{1,0:T(8,128)(2,1)S(1)}, bf16[32,3072]{1,0:T(8,128)(2,1)S(1)}, u32[]{:S(2)}, u32[]{:S(2)}) collective-permute-start(bf16[32,3072]{1,0:T(8,128)(2,1)S(1)} %convert_select_fusion.4), channel_id=1, source_target_pairs={{0,8},{1,9},{2,10},{3,11},{4,12},{5,13},{6,14},{7,15},{16,24},{17,... | collective-permute-start | bytes 589832 | tf_op jit(solution)/shard_map/while/body/eval_jaxpr/ppermute | solution.py:26
  (41 other events, 397.6 us)
Sparse Core Ops, SparseCore 0:
  619.2 66.1 reduce-scatter.1
where the time goes:
time: 694 us; the launch traced here: 692 us
  waiting for transfers between devices  351 us (51%)
  starting transfers between devices  121 us (17%)
  matrix products  75.3 us (11%)
  blocking collectives  41.6 us (6%)
  local copies, waits for them, and re-layouts  38.4 us (6%)
  other arithmetic  37.4 us (5%)
  between operations  13.5 us (2%)
  loops' own time  13 us (2%)
    ppermute x30, waiting for transfers between devices, from_partner(): lax.ppermute(value, axis, [(i, i ^ 1 << distance) for i in range(lax.axis...  261 us
    reduce_scatter x1, waiting for transfers between devices, on_device(): lax.psum_scatter(finished[3][:seq_rows], 'section', scatter_dimension=0,...  66.3 us
    ppermute x30, starting transfers between devices, from_partner(): lax.ppermute(value, axis, [(i, i ^ 1 << distance) for i in range(lax.axis...  64 us
    ppermute x10, starting transfers between devices, from_behind(): lax.ppermute(value, axis, [(source, source + steps) for source in range(l...  57.5 us
    dot_general x4, matrix products, attend_group(): jnp.dot(modded, w_qkv, preferred_element_type=jnp.float32)  24.9 us
    ppermute x10, waiting for transfers between devices, from_behind(): lax.ppermute(value, axis, [(source, source + steps) for source in range(l...  23.8 us
    all_gather x1, blocking collectives, on_device(): lax.all_gather(latent, 'section', axis=0, tiled=True)  23.6 us
    all_gather x1, blocking collectives, on_device(): lax.all_gather(control_latent, 'section', axis=0, tiled=True)  17.9 us
  transfers between devices with their start and end apart: 41, of which 41 were waited for; matrix products, arithmetic and copies ran while one was open for 2% of the time, Pallas kernels for 0%

commit v1 on v0

--- a/solution.py
+++ b/solution.py
@@ -14,6 +14,18 @@
 TILES = 6
 PMAX = 2
 EPSILON = 1e-06
+
+
+def doubled_up(x, axis, dim):
+    ways, here = (lax.axis_size(axis), lax.axis_index(axis))
+    grown, reach = (x, 1)
+    while reach < ways:
+        theirs = lax.ppermute(grown, axis, [(d, d ^ reach) for d in range(ways)])
+        mine_first = jnp.concatenate([grown, theirs], axis=dim)
+        theirs_first = jnp.concatenate([theirs, grown], axis=dim)
+        grown = jnp.where(here & reach == 0, mine_first, theirs_first)
+        reach = 2 * reach
+    return grown
 
 
 def from_partner(value, axis, distance):
@@ -129,7 +141,7 @@
         share_start = share_start + (group_index >> bit_index & 1) * (row_count >> position + 1)
     whole_latent, whole_control = (
         lax.all_gather(latent, "section", axis=0, tiled=True),
-        lax.all_gather(control_latent, "section", axis=0, tiled=True),
+        doubled_up(control_latent, "section", 0),
     )
     padding = ((0, row_count), (0, 0))
     latent_pad = jnp.pad(whole_latent, padding)

time: 694 us -> 686 us (0.988)
  blocking collectives: 41.6 us -> 20.1 us
  waiting for transfers between devices: 351 us -> 360 us
    all_gather x1 -> x0, blocking collectives: 17.9 us -> none  [on_device(): lax.all_gather(control_latent, 'section', axis=0, tiled=True)]
    ppermute x0 -> x4, starting transfers between devices: none -> 8.32 us  [doubled_up(): theirs = lax.ppermute(grown, axis, [(d, d ^ reach) for d in range(ways)])]
  transfers between devices with their start and end apart: 41 -> 45, of which waited for: 41 -> 43; matrix products, arithmetic and copies ran while one was open for 2% -> 3% of each run, Pallas kernels for 0% -> 0%
where the time goes in v1:
time: 686 us; the launch traced here: 684 us
  waiting for transfers between devices  360 us (52%)
  starting transfers between devices  123 us (18%)
  matrix products  74.9 us (11%)
  local copies, waits for them, and re-layouts  40.3 us (6%)
  other arithmetic  39.6 us (6%)
  blocking collectives  20.1 us (3%)
  between operations  13.5 us (2%)
  loops' own time  13.1 us (2%)
    ppermute x30, waiting for transfers between devices, from_partner(): lax.ppermute(value, axis, [(i, i ^ 1 << distance) for i in range(lax.axis...  268 us
    reduce_scatter x1, waiting for transfers between devices, on_device(): lax.psum_scatter(finished[3][:seq_rows], 'section', scatter_dimension=0,...  65.7 us
    ppermute x10, starting transfers between devices, from_behind(): lax.ppermute(value, axis, [(source, source + steps) for source in range(l...  57.3 us
    ppermute x30, starting transfers between devices, from_partner(): lax.ppermute(value, axis, [(i, i ^ 1 << distance) for i in range(lax.axis...  57.1 us
    dot_general x4, matrix products, attend_group(): jnp.dot(modded, w_qkv, preferred_element_type=jnp.float32)  24.5 us
    ppermute x10, waiting for transfers between devices, from_behind(): lax.ppermute(value, axis, [(source, source + steps) for source in range(l...  23.8 us
    all_gather x1, blocking collectives, on_device(): lax.all_gather(latent, 'section', axis=0, tiled=True)  20.1 us
    dot_general x4, matrix products, attend_group(): jnp.einsum('thqk,tkhd->tqhd', probabilities, value_rows, preferred_elemen...  14 us
  transfers between devices with their start and end apart: 45, of which 43 were waited for; matrix products, arithmetic and copies ran while one was open for 3% of the time, Pallas kernels for 0%

profile of v1, /device:TPU:0, one launch (start us, length us, event | category | flops | bytes accessed | tf_op | source)
XLA Modules:
  0.0 684.5 jit_solution(920171735411542106)
XLA Ops:
  24.9 20.1 %all_gather.3 = bf16[768,64]{1,0:T(8,128)(2,1)S(1)} all-gather(bf16[48,64]{1,0:T(8,128)(2,1)S(1)} %copy-done.7), channel_id=1, replica_groups=mesh['grp'=2,'section'=16] {'section'}, dimensions={0}, use_global_device_ids=true | all-gather | bytes 104448 | tf_op jit(solution)/shard_map/all_gather | solution.py:143
  48.1 562.0 %while.25 = (s32[]{:T(128)}, bf16[32,3072]{1,0:T(8,128)(2,1)}, bf16[32,3072]{1,0:T(8,128)(2,1)S(1)}, bf16[1024,768]{0,1:T(8,128)(2,1)}, f32[1024,64]{1,0:T(8,128...) while((s32[]{:T(128)}, bf16[32,3072]{1,0:T(8,128)(2,1)}, ...), condition=%wide.region_12.13_spmd, body=%wide.region_1.12_spmd.sunk | while | flops 2714486016 | bytes 100601624 | solution.py:254
  54.1 11.4 %collective-permute-done.1 = bf16[64,3072]{1,0:T(8,128)(2,1)S(1)} collective-permute-done((bf16[64,3072]{1,0:T(8,128)(2,1)S(1)}, bf16[64,3072]{1,0:T(8,128)(2,1)S(1)}, u32[]{:S(2)}, u32[]{:S(2)}) %collective-permute-start.1) | collective-permute-done | bytes 393248 | tf_op jit(solution)/shard_map/while/body/eval_jaxpr/ppermute | solution.py:32
  66.5 18.2 %collective-permute-done.2 = bf16[128,3072]{1,0:T(8,128)(2,1)} collective-permute-done((bf16[128,3072]{1,0:T(8,128)(2,1)S(1)}, bf16[128,3072]{1,0:T(8,128)(2,1)}, u32[]{:S(2)}, u32[]{:S(2)}) %collective-permute-start.2) | collective-permute-done | bytes 786464 | tf_op jit(solution)/shard_map/while/body/eval_jaxpr/ppermute | solution.py:32
  86.8 25.0 %conditional.2 = (bf16[1024,768]{0,1:T(8,128)(2,1)}, bf16[128,3072]{1,0:T(8,128)(2,1)S(1)}, bf16[128,3072]{1,0:T(8,128)(2,1)S(1)}) conditional(s32[]{:T(128)} %convert_element_type.288, bf16[1024,768]{0,1:T(8,128)(2,1)} %get-tuple-element.1047, (s32[]{:T(128)}, pred[]{:T(512)}, bf16[256,3072]{1,0:T(8,128)(2,1)S(1)}, bf16[256,3072]{1,0:T(8,128)(2,1)S(1)}, ...), branch_computations={%region_2.2_spmd, %region_3.9_spmd} | conditional | flops 2658447616 | bytes 57946768 | solution.py:223
  112.2 17.8 %collective-permute-done.3 = bf16[128,3072]{1,0:T(8,128)(2,1)S(1)} collective-permute-done((bf16[128,3072]{1,0:T(8,128)(2,1)S(1)}, bf16[128,3072]{1,0:T(8,128)(2,1)S(1)}, u32[]{:S(2)}, u32[]{:S(2)}) %collective-permute-start.3) | collective-permute-done | bytes 786464 | tf_op jit(solution)/shard_map/while/body/eval_jaxpr/ppermute | solution.py:32
  131.3 7.9 %collective-permute-done.4 = bf16[64,3072]{1,0:T(8,128)(2,1)S(1)} collective-permute-done((bf16[64,3072]{1,0:T(8,128)(2,1)S(1)}, bf16[64,3072]{1,0:T(8,128)(2,1)S(1)}, u32[]{:S(2)}, u32[]{:S(2)}) %collective-permute-start.4) | collective-permute-done | bytes 393248 | tf_op jit(solution)/shard_map/while/body/eval_jaxpr/ppermute | solution.py:32
  158.6 10.0 %collective-permute-done.1 = bf16[64,3072]{1,0:T(8,128)(2,1)S(1)} collective-permute-done((bf16[64,3072]{1,0:T(8,128)(2,1)S(1)}, bf16[64,3072]{1,0:T(8,128)(2,1)S(1)}, u32[]{:S(2)}, u32[]{:S(2)}) %collective-permute-start.1) | collective-permute-done | bytes 393248 | tf_op jit(solution)/shard_map/while/body/eval_jaxpr/ppermute | solution.py:32
  168.8 9.3 %collective-permute-start.2 = (bf16[128,3072]{1,0:T(8,128)(2,1)S(1)}, bf16[128,3072]{1,0:T(8,128)(2,1)}, u32[]{:S(2)}, u32[]{:S(2)}) collective-permute-start(bf16[128,3072]{1,0:T(8,128)(2,1)S(1)} %maximum_select_fusion.10), channel_id=1, source_target_pairs={{0,4},{1,5},{2,6},{3,7},{4,0},{5,1},{6,2},{7,3},{8,12},{9,13},{10,... | collective-permute-start | bytes 2359304 | tf_op jit(solution)/shard_map/while/body/eval_jaxpr/ppermute | solution.py:32
  178.8 16.4 %collective-permute-done.2 = bf16[128,3072]{1,0:T(8,128)(2,1)} collective-permute-done((bf16[128,3072]{1,0:T(8,128)(2,1)S(1)}, bf16[128,3072]{1,0:T(8,128)(2,1)}, u32[]{:S(2)}, u32[]{:S(2)}) %collective-permute-start.2) | collective-permute-done | bytes 786464 | tf_op jit(solution)/shard_map/while/body/eval_jaxpr/ppermute | solution.py:32
  197.3 25.0 %conditional.2 = (bf16[1024,768]{0,1:T(8,128)(2,1)}, bf16[128,3072]{1,0:T(8,128)(2,1)S(1)}, bf16[128,3072]{1,0:T(8,128)(2,1)S(1)}) conditional(s32[]{:T(128)} %convert_element_type.288, bf16[1024,768]{0,1:T(8,128)(2,1)} %get-tuple-element.1047, (s32[]{:T(128)}, pred[]{:T(512)}, bf16[256,3072]{1,0:T(8,128)(2,1)S(1)}, bf16[256,3072]{1,0:T(8,128)(2,1)S(1)}, ...), branch_computations={%region_2.2_spmd, %region_3.9_spmd} | conditional | flops 2658447616 | bytes 57946768 | solution.py:223
  224.2 16.4 %collective-permute-done.3 = bf16[128,3072]{1,0:T(8,128)(2,1)S(1)} collective-permute-done((bf16[128,3072]{1,0:T(8,128)(2,1)S(1)}, bf16[128,3072]{1,0:T(8,128)(2,1)S(1)}, u32[]{:S(2)}, u32[]{:S(2)}) %collective-permute-start.3) | collective-permute-done | bytes 786464 | tf_op jit(solution)/shard_map/while/body/eval_jaxpr/ppermute | solution.py:32
  242.2 7.7 %collective-permute-done.4 = bf16[64,3072]{1,0:T(8,128)(2,1)S(1)} collective-permute-done((bf16[64,3072]{1,0:T(8,128)(2,1)S(1)}, bf16[64,3072]{1,0:T(8,128)(2,1)S(1)}, u32[]{:S(2)}, u32[]{:S(2)}) %collective-permute-start.4) | collective-permute-done | bytes 393248 | tf_op jit(solution)/shard_map/while/body/eval_jaxpr/ppermute | solution.py:32
  273.0 10.0 %collective-permute-done.1 = bf16[64,3072]{1,0:T(8,128)(2,1)S(1)} collective-permute-done((bf16[64,3072]{1,0:T(8,128)(2,1)S(1)}, bf16[64,3072]{1,0:T(8,128)(2,1)S(1)}, u32[]{:S(2)}, u32[]{:S(2)}) %collective-permute-start.1) | collective-permute-done | bytes 393248 | tf_op jit(solution)/shard_map/while/body/eval_jaxpr/ppermute | solution.py:32
  283.2 9.6 %collective-permute-start.2 = (bf16[128,3072]{1,0:T(8,128)(2,1)S(1)}, bf16[128,3072]{1,0:T(8,128)(2,1)}, u32[]{:S(2)}, u32[]{:S(2)}) collective-permute-start(bf16[128,3072]{1,0:T(8,128)(2,1)S(1)} %maximum_select_fusion.10), channel_id=1, source_target_pairs={{0,4},{1,5},{2,6},{3,7},{4,0},{5,1},{6,2},{7,3},{8,12},{9,13},{10,... | collective-permute-start | bytes 2359304 | tf_op jit(solution)/shard_map/while/body/eval_jaxpr/ppermute | solution.py:32
  293.5 16.4 %collective-permute-done.2 = bf16[128,3072]{1,0:T(8,128)(2,1)} collective-permute-done((bf16[128,3072]{1,0:T(8,128)(2,1)S(1)}, bf16[128,3072]{1,0:T(8,128)(2,1)}, u32[]{:S(2)}, u32[]{:S(2)}) %collective-permute-start.2) | collective-permute-done | bytes 786464 | tf_op jit(solution)/shard_map/while/body/eval_jaxpr/ppermute | solution.py:32
  312.0 25.0 %conditional.2 = (bf16[1024,768]{0,1:T(8,128)(2,1)}, bf16[128,3072]{1,0:T(8,128)(2,1)S(1)}, bf16[128,3072]{1,0:T(8,128)(2,1)S(1)}) conditional(s32[]{:T(128)} %convert_element_type.288, bf16[1024,768]{0,1:T(8,128)(2,1)} %get-tuple-element.1047, (s32[]{:T(128)}, pred[]{:T(512)}, bf16[256,3072]{1,0:T(8,128)(2,1)S(1)}, bf16[256,3072]{1,0:T(8,128)(2,1)S(1)}, ...), branch_computations={%region_2.2_spmd, %region_3.9_spmd} | conditional | flops 2658447616 | bytes 57946768 | solution.py:223
  338.9 16.4 %collective-permute-done.3 = bf16[128,3072]{1,0:T(8,128)(2,1)S(1)} collective-permute-done((bf16[128,3072]{1,0:T(8,128)(2,1)S(1)}, bf16[128,3072]{1,0:T(8,128)(2,1)S(1)}, u32[]{:S(2)}, u32[]{:S(2)}) %collective-permute-start.3) | collective-permute-done | bytes 786464 | tf_op jit(solution)/shard_map/while/body/eval_jaxpr/ppermute | solution.py:32
  356.9 7.7 %collective-permute-done.4 = bf16[64,3072]{1,0:T(8,128)(2,1)S(1)} collective-permute-done((bf16[64,3072]{1,0:T(8,128)(2,1)S(1)}, bf16[64,3072]{1,0:T(8,128)(2,1)S(1)}, u32[]{:S(2)}, u32[]{:S(2)}) %collective-permute-start.4) | collective-permute-done | bytes 393248 | tf_op jit(solution)/shard_map/while/body/eval_jaxpr/ppermute | solution.py:32
  387.7 10.0 %collective-permute-done.1 = bf16[64,3072]{1,0:T(8,128)(2,1)S(1)} collective-permute-done((bf16[64,3072]{1,0:T(8,128)(2,1)S(1)}, bf16[64,3072]{1,0:T(8,128)(2,1)S(1)}, u32[]{:S(2)}, u32[]{:S(2)}) %collective-permute-start.1) | collective-permute-done | bytes 393248 | tf_op jit(solution)/shard_map/while/body/eval_jaxpr/ppermute | solution.py:32
  397.9 9.6 %collective-permute-start.2 = (bf16[128,3072]{1,0:T(8,128)(2,1)S(1)}, bf16[128,3072]{1,0:T(8,128)(2,1)}, u32[]{:S(2)}, u32[]{:S(2)}) collective-permute-start(bf16[128,3072]{1,0:T(8,128)(2,1)S(1)} %maximum_select_fusion.10), channel_id=1, source_target_pairs={{0,4},{1,5},{2,6},{3,7},{4,0},{5,1},{6,2},{7,3},{8,12},{9,13},{10,... | collective-permute-start | bytes 2359304 | tf_op jit(solution)/shard_map/while/body/eval_jaxpr/ppermute | solution.py:32
  408.2 16.4 %collective-permute-done.2 = bf16[128,3072]{1,0:T(8,128)(2,1)} collective-permute-done((bf16[128,3072]{1,0:T(8,128)(2,1)S(1)}, bf16[128,3072]{1,0:T(8,128)(2,1)}, u32[]{:S(2)}, u32[]{:S(2)}) %collective-permute-start.2) | collective-permute-done | bytes 786464 | tf_op jit(solution)/shard_map/while/body/eval_jaxpr/ppermute | solution.py:32
  426.7 25.0 %conditional.2 = (bf16[1024,768]{0,1:T(8,128)(2,1)}, bf16[128,3072]{1,0:T(8,128)(2,1)S(1)}, bf16[128,3072]{1,0:T(8,128)(2,1)S(1)}) conditional(s32[]{:T(128)} %convert_element_type.288, bf16[1024,768]{0,1:T(8,128)(2,1)} %get-tuple-element.1047, (s32[]{:T(128)}, pred[]{:T(512)}, bf16[256,3072]{1,0:T(8,128)(2,1)S(1)}, bf16[256,3072]{1,0:T(8,128)(2,1)S(1)}, ...), branch_computations={%region_2.2_spmd, %region_3.9_spmd} | conditional | flops 2658447616 | bytes 57946768 | solution.py:223
  453.6 16.4 %collective-permute-done.3 = bf16[128,3072]{1,0:T(8,128)(2,1)S(1)} collective-permute-done((bf16[128,3072]{1,0:T(8,128)(2,1)S(1)}, bf16[128,3072]{1,0:T(8,128)(2,1)S(1)}, u32[]{:S(2)}, u32[]{:S(2)}) %collective-permute-start.3) | collective-permute-done | bytes 786464 | tf_op jit(solution)/shard_map/while/body/eval_jaxpr/ppermute | solution.py:32
  471.7 7.7 %collective-permute-done.4 = bf16[64,3072]{1,0:T(8,128)(2,1)S(1)} collective-permute-done((bf16[64,3072]{1,0:T(8,128)(2,1)S(1)}, bf16[64,3072]{1,0:T(8,128)(2,1)S(1)}, u32[]{:S(2)}, u32[]{:S(2)}) %collective-permute-start.4) | collective-permute-done | bytes 393248 | tf_op jit(solution)/shard_map/while/body/eval_jaxpr/ppermute | solution.py:32
  502.5 10.0 %collective-permute-done.1 = bf16[64,3072]{1,0:T(8,128)(2,1)S(1)} collective-permute-done((bf16[64,3072]{1,0:T(8,128)(2,1)S(1)}, bf16[64,3072]{1,0:T(8,128)(2,1)S(1)}, u32[]{:S(2)}, u32[]{:S(2)}) %collective-permute-start.1) | collective-permute-done | bytes 393248 | tf_op jit(solution)/shard_map/while/body/eval_jaxpr/ppermute | solution.py:32
  512.6 9.6 %collective-permute-start.2 = (bf16[128,3072]{1,0:T(8,128)(2,1)S(1)}, bf16[128,3072]{1,0:T(8,128)(2,1)}, u32[]{:S(2)}, u32[]{:S(2)}) collective-permute-start(bf16[128,3072]{1,0:T(8,128)(2,1)S(1)} %maximum_select_fusion.10), channel_id=1, source_target_pairs={{0,4},{1,5},{2,6},{3,7},{4,0},{5,1},{6,2},{7,3},{8,12},{9,13},{10,... | collective-permute-start | bytes 2359304 | tf_op jit(solution)/shard_map/while/body/eval_jaxpr/ppermute | solution.py:32
  522.9 16.4 %collective-permute-done.2 = bf16[128,3072]{1,0:T(8,128)(2,1)} collective-permute-done((bf16[128,3072]{1,0:T(8,128)(2,1)S(1)}, bf16[128,3072]{1,0:T(8,128)(2,1)}, u32[]{:S(2)}, u32[]{:S(2)}) %collective-permute-start.2) | collective-permute-done | bytes 786464 | tf_op jit(solution)/shard_map/while/body/eval_jaxpr/ppermute | solution.py:32
  543.5 16.4 %collective-permute-done.3 = bf16[128,3072]{1,0:T(8,128)(2,1)S(1)} collective-permute-done((bf16[128,3072]{1,0:T(8,128)(2,1)S(1)}, bf16[128,3072]{1,0:T(8,128)(2,1)S(1)}, u32[]{:S(2)}, u32[]{:S(2)}) %collective-permute-start.3) | collective-permute-done | bytes 786464 | tf_op jit(solution)/shard_map/while/body/eval_jaxpr/ppermute | solution.py:32
  561.5 7.7 %collective-permute-done.4 = bf16[64,3072]{1,0:T(8,128)(2,1)S(1)} collective-permute-done((bf16[64,3072]{1,0:T(8,128)(2,1)S(1)}, bf16[64,3072]{1,0:T(8,128)(2,1)S(1)}, u32[]{:S(2)}, u32[]{:S(2)}) %collective-permute-start.4) | collective-permute-done | bytes 393248 | tf_op jit(solution)/shard_map/while/body/eval_jaxpr/ppermute | solution.py:32
  571.2 30.9 %collective-permute-start.6 = (bf16[32,3072]{1,0:T(8,128)(2,1)S(1)}, bf16[32,3072]{1,0:T(8,128)(2,1)}, u32[]{:S(2)}, u32[]{:S(2)}) collective-permute-start(bf16[32,3072]{1,0:T(8,128)(2,1)S(1)} %get-tuple-element.999), channel_id=1, source_target_pairs={{0,8},{1,9},{2,10},{3,11},{4,12},{5,13},{6,14},{7,15},{16,24},{17,... | collective-permute-start | bytes 589832 | tf_op jit(solution)/shard_map/while/body/eval_jaxpr/ppermute | solution.py:38
  611.9 65.7 %reduce-scatter.2.cloned.1.call-done = f32[48,64]{1,0:T(8,128)} async-done(((f32[768,64]{1,0:T(8,128)}), f32[48,64]{1,0:T(8,128)}) %reduce-scatter.2.cloned.1.call-update) | async-done | bytes 12304 | tf_op jit(solution)/shard_map/reduce_scatter | solution.py:255
  (397 shorter events, 245.5 us)
Async XLA Ops:
  6.5 671.1 %reduce-scatter.2.cloned.1.call-start = ((), (), s32[]{:S(2)}) async-start(), calls=%async_computation.1 | async-start | bytes 417792 | tf_op jit(solution)/shard_map/reduce_scatter | solution.py:255
  18.1 27.7 %collective-permute-start.11 = (bf16[384,64]{1,0:T(8,128)(2,1)S(1)}, bf16[384,64]{1,0:T(8,128)(2,1)S(1)}, u32[]{:S(2)}, u32[]{:S(2)}) collective-permute-start(bf16[384,64]{1,0:T(8,128)(2,1)S(1)} %maximum_select_fusion.4), channel_id=1, source_target_pairs={{0,8},{1,9},{2,10},{3,11},{4,12},{5,13},{6,14},{7,15},{8,0},{9,1},... | collective-permute-start | bytes 147464 | tf_op jit(solution)/shard_map/ppermute | solution.py:23
  54.0 11.4 %collective-permute-start.1 = (bf16[64,3072]{1,0:T(8,128)(2,1)S(1)}, bf16[64,3072]{1,0:T(8,128)(2,1)S(1)}, u32[]{:S(2)}, u32[]{:S(2)}) collective-permute-start(bf16[64,3072]{1,0:T(8,128)(2,1)S(1)} %maximum_select_fusion.9), channel_id=1, source_target_pairs={{0,2},{1,3},{2,0},{3,1},{4,6},{5,7},{6,4},{7,5},{8,10},{9,11},{10,... | collective-permute-start | bytes 1179656 | tf_op jit(solution)/shard_map/while/body/eval_jaxpr/ppermute | solution.py:32
  65.6 19.1 %collective-permute-start.2 = (bf16[128,3072]{1,0:T(8,128)(2,1)S(1)}, bf16[128,3072]{1,0:T(8,128)(2,1)}, u32[]{:S(2)}, u32[]{:S(2)}) collective-permute-start(bf16[128,3072]{1,0:T(8,128)(2,1)S(1)} %maximum_select_fusion.10), channel_id=1, source_target_pairs={{0,4},{1,5},{2,6},{3,7},{4,0},{5,1},{6,2},{7,3},{8,12},{9,13},{10,... | collective-permute-start | bytes 2359304 | tf_op jit(solution)/shard_map/while/body/eval_jaxpr/ppermute | solution.py:32
  111.9 18.1 %collective-permute-start.3 = (bf16[128,3072]{1,0:T(8,128)(2,1)S(1)}, bf16[128,3072]{1,0:T(8,128)(2,1)S(1)}, u32[]{:S(2)}, u32[]{:S(2)}) collective-permute-start(bf16[128,3072]{1,0:T(8,128)(2,1)S(1)} %broadcast_select_fusion.7), channel_id=1, source_target_pairs={{0,4},{1,5},{2,6},{3,7},{4,0},{5,1},{6,2},{7,3},{8,12},{9,13},{10,... | collective-permute-start | bytes 2359304 | tf_op jit(solution)/shard_map/while/body/eval_jaxpr/ppermute | solution.py:32
  130.4 8.9 %collective-permute-start.4 = (bf16[64,3072]{1,0:T(8,128)(2,1)S(1)}, bf16[64,3072]{1,0:T(8,128)(2,1)S(1)}, u32[]{:S(2)}, u32[]{:S(2)}) collective-permute-start(bf16[64,3072]{1,0:T(8,128)(2,1)S(1)} %select_convert_fusion.4), channel_id=1, source_target_pairs={{0,2},{1,3},{2,0},{3,1},{4,6},{5,7},{6,4},{7,5},{8,10},{9,11},{10,... | collective-permute-start | bytes 1179656 | tf_op jit(solution)/shard_map/while/body/eval_jaxpr/ppermute | solution.py:32
  141.3 6.6 collective-permute-start.6
  143.4 8.2 %collective-permute-start.7 = (bf16[32,3072]{1,0:T(8,128)(2,1)S(1)}, bf16[32,3072]{1,0:T(8,128)(2,1)S(1)}, u32[]{:S(2)}, u32[]{:S(2)}) collective-permute-start(bf16[32,3072]{1,0:T(8,128)(2,1)S(1)} %convert_select_fusion.4), channel_id=1, source_target_pairs={{0,8},{1,9},{2,10},{3,11},{4,12},{5,13},{6,14},{7,15},{16,24},{17,... | collective-permute-start | bytes 589832 | tf_op jit(solution)/shard_map/while/body/eval_jaxpr/ppermute | solution.py:38
  157.4 11.2 %collective-permute-start.1 = (bf16[64,3072]{1,0:T(8,128)(2,1)S(1)}, bf16[64,3072]{1,0:T(8,128)(2,1)S(1)}, u32[]{:S(2)}, u32[]{:S(2)}) collective-permute-start(bf16[64,3072]{1,0:T(8,128)(2,1)S(1)} %maximum_select_fusion.9), channel_id=1, source_target_pairs={{0,2},{1,3},{2,0},{3,1},{4,6},{5,7},{6,4},{7,5},{8,10},{9,11},{10,... | collective-permute-start | bytes 1179656 | tf_op jit(solution)/shard_map/while/body/eval_jaxpr/ppermute | solution.py:32
  168.8 26.4 %collective-permute-start.2 = (bf16[128,3072]{1,0:T(8,128)(2,1)S(1)}, bf16[128,3072]{1,0:T(8,128)(2,1)}, u32[]{:S(2)}, u32[]{:S(2)}) collective-permute-start(bf16[128,3072]{1,0:T(8,128)(2,1)S(1)} %maximum_select_fusion.10), channel_id=1, source_target_pairs={{0,4},{1,5},{2,6},{3,7},{4,0},{5,1},{6,2},{7,3},{8,12},{9,13},{10,... | collective-permute-start | bytes 2359304 | tf_op jit(solution)/shard_map/while/body/eval_jaxpr/ppermute | solution.py:32
  222.3 18.2 %collective-permute-start.3 = (bf16[128,3072]{1,0:T(8,128)(2,1)S(1)}, bf16[128,3072]{1,0:T(8,128)(2,1)S(1)}, u32[]{:S(2)}, u32[]{:S(2)}) collective-permute-start(bf16[128,3072]{1,0:T(8,128)(2,1)S(1)} %broadcast_select_fusion.7), channel_id=1, source_target_pairs={{0,4},{1,5},{2,6},{3,7},{4,0},{5,1},{6,2},{7,3},{8,12},{9,13},{10,... | collective-permute-start | bytes 2359304 | tf_op jit(solution)/shard_map/while/body/eval_jaxpr/ppermute | solution.py:32
  241.0 8.9 %collective-permute-start.4 = (bf16[64,3072]{1,0:T(8,128)(2,1)S(1)}, bf16[64,3072]{1,0:T(8,128)(2,1)S(1)}, u32[]{:S(2)}, u32[]{:S(2)}) collective-permute-start(bf16[64,3072]{1,0:T(8,128)(2,1)S(1)} %select_convert_fusion.4), channel_id=1, source_target_pairs={{0,2},{1,3},{2,0},{3,1},{4,6},{5,7},{6,4},{7,5},{8,10},{9,11},{10,... | collective-permute-start | bytes 1179656 | tf_op jit(solution)/shard_map/while/body/eval_jaxpr/ppermute | solution.py:32
  251.9 10.7 %collective-permute-start.6 = (bf16[32,3072]{1,0:T(8,128)(2,1)S(1)}, bf16[32,3072]{1,0:T(8,128)(2,1)}, u32[]{:S(2)}, u32[]{:S(2)}) collective-permute-start(bf16[32,3072]{1,0:T(8,128)(2,1)S(1)} %get-tuple-element.999), channel_id=1, source_target_pairs={{0,8},{1,9},{2,10},{3,11},{4,12},{5,13},{6,14},{7,15},{16,24},{17,... | collective-permute-start | bytes 589832 | tf_op jit(solution)/shard_map/while/body/eval_jaxpr/ppermute | solution.py:38
  258.0 7.9 %collective-permute-start.7 = (bf16[32,3072]{1,0:T(8,128)(2,1)S(1)}, bf16[32,3072]{1,0:T(8,128)(2,1)S(1)}, u32[]{:S(2)}, u32[]{:S(2)}) collective-permute-start(bf16[32,3072]{1,0:T(8,128)(2,1)S(1)} %convert_select_fusion.4), channel_id=1, source_target_pairs={{0,8},{1,9},{2,10},{3,11},{4,12},{5,13},{6,14},{7,15},{16,24},{17,... | collective-permute-start | bytes 589832 | tf_op jit(solution)/shard_map/while/body/eval_jaxpr/ppermute | solution.py:38
  271.8 11.2 %collective-permute-start.1 = (bf16[64,3072]{1,0:T(8,128)(2,1)S(1)}, bf16[64,3072]{1,0:T(8,128)(2,1)S(1)}, u32[]{:S(2)}, u32[]{:S(2)}) collective-permute-start(bf16[64,3072]{1,0:T(8,128)(2,1)S(1)} %maximum_select_fusion.9), channel_id=1, source_target_pairs={{0,2},{1,3},{2,0},{3,1},{4,6},{5,7},{6,4},{7,5},{8,10},{9,11},{10,... | collective-permute-start | bytes 1179656 | tf_op jit(solution)/shard_map/while/body/eval_jaxpr/ppermute | solution.py:32
  283.2 26.7 %collective-permute-start.2 = (bf16[128,3072]{1,0:T(8,128)(2,1)S(1)}, bf16[128,3072]{1,0:T(8,128)(2,1)}, u32[]{:S(2)}, u32[]{:S(2)}) collective-permute-start(bf16[128,3072]{1,0:T(8,128)(2,1)S(1)} %maximum_select_fusion.10), channel_id=1, source_target_pairs={{0,4},{1,5},{2,6},{3,7},{4,0},{5,1},{6,2},{7,3},{8,12},{9,13},{10,... | collective-permute-start | bytes 2359304 | tf_op jit(solution)/shard_map/while/body/eval_jaxpr/ppermute | solution.py:32
  337.1 18.2 %collective-permute-start.3 = (bf16[128,3072]{1,0:T(8,128)(2,1)S(1)}, bf16[128,3072]{1,0:T(8,128)(2,1)S(1)}, u32[]{:S(2)}, u32[]{:S(2)}) collective-permute-start(bf16[128,3072]{1,0:T(8,128)(2,1)S(1)} %broadcast_select_fusion.7), channel_id=1, source_target_pairs={{0,4},{1,5},{2,6},{3,7},{4,0},{5,1},{6,2},{7,3},{8,12},{9,13},{10,... | collective-permute-start | bytes 2359304 | tf_op jit(solution)/shard_map/while/body/eval_jaxpr/ppermute | solution.py:32
  355.7 8.9 %collective-permute-start.4 = (bf16[64,3072]{1,0:T(8,128)(2,1)S(1)}, bf16[64,3072]{1,0:T(8,128)(2,1)S(1)}, u32[]{:S(2)}, u32[]{:S(2)}) collective-permute-start(bf16[64,3072]{1,0:T(8,128)(2,1)S(1)} %select_convert_fusion.4), channel_id=1, source_target_pairs={{0,2},{1,3},{2,0},{3,1},{4,6},{5,7},{6,4},{7,5},{8,10},{9,11},{10,... | collective-permute-start | bytes 1179656 | tf_op jit(solution)/shard_map/while/body/eval_jaxpr/ppermute | solution.py:32
  366.6 10.6 %collective-permute-start.6 = (bf16[32,3072]{1,0:T(8,128)(2,1)S(1)}, bf16[32,3072]{1,0:T(8,128)(2,1)}, u32[]{:S(2)}, u32[]{:S(2)}) collective-permute-start(bf16[32,3072]{1,0:T(8,128)(2,1)S(1)} %get-tuple-element.999), channel_id=1, source_target_pairs={{0,8},{1,9},{2,10},{3,11},{4,12},{5,13},{6,14},{7,15},{16,24},{17,... | collective-permute-start | bytes 589832 | tf_op jit(solution)/shard_map/while/body/eval_jaxpr/ppermute | solution.py:38
  372.7 7.9 %collective-permute-start.7 = (bf16[32,3072]{1,0:T(8,128)(2,1)S(1)}, bf16[32,3072]{1,0:T(8,128)(2,1)S(1)}, u32[]{:S(2)}, u32[]{:S(2)}) collective-permute-start(bf16[32,3072]{1,0:T(8,128)(2,1)S(1)} %convert_select_fusion.4), channel_id=1, source_target_pairs={{0,8},{1,9},{2,10},{3,11},{4,12},{5,13},{6,14},{7,15},{16,24},{17,... | collective-permute-start | bytes 589832 | tf_op jit(solution)/shard_map/while/body/eval_jaxpr/ppermute | solution.py:38
  386.5 11.2 %collective-permute-start.1 = (bf16[64,3072]{1,0:T(8,128)(2,1)S(1)}, bf16[64,3072]{1,0:T(8,128)(2,1)S(1)}, u32[]{:S(2)}, u32[]{:S(2)}) collective-permute-start(bf16[64,3072]{1,0:T(8,128)(2,1)S(1)} %maximum_select_fusion.9), channel_id=1, source_target_pairs={{0,2},{1,3},{2,0},{3,1},{4,6},{5,7},{6,4},{7,5},{8,10},{9,11},{10,... | collective-permute-start | bytes 1179656 | tf_op jit(solution)/shard_map/while/body/eval_jaxpr/ppermute | solution.py:32
  397.9 26.7 %collective-permute-start.2 = (bf16[128,3072]{1,0:T(8,128)(2,1)S(1)}, bf16[128,3072]{1,0:T(8,128)(2,1)}, u32[]{:S(2)}, u32[]{:S(2)}) collective-permute-start(bf16[128,3072]{1,0:T(8,128)(2,1)S(1)} %maximum_select_fusion.10), channel_id=1, source_target_pairs={{0,4},{1,5},{2,6},{3,7},{4,0},{5,1},{6,2},{7,3},{8,12},{9,13},{10,... | collective-permute-start | bytes 2359304 | tf_op jit(solution)/shard_map/while/body/eval_jaxpr/ppermute | solution.py:32
  451.8 18.2 %collective-permute-start.3 = (bf16[128,3072]{1,0:T(8,128)(2,1)S(1)}, bf16[128,3072]{1,0:T(8,128)(2,1)S(1)}, u32[]{:S(2)}, u32[]{:S(2)}) collective-permute-start(bf16[128,3072]{1,0:T(8,128)(2,1)S(1)} %broadcast_select_fusion.7), channel_id=1, source_target_pairs={{0,4},{1,5},{2,6},{3,7},{4,0},{5,1},{6,2},{7,3},{8,12},{9,13},{10,... | collective-permute-start | bytes 2359304 | tf_op jit(solution)/shard_map/while/body/eval_jaxpr/ppermute | solution.py:32
  470.4 8.9 %collective-permute-start.4 = (bf16[64,3072]{1,0:T(8,128)(2,1)S(1)}, bf16[64,3072]{1,0:T(8,128)(2,1)S(1)}, u32[]{:S(2)}, u32[]{:S(2)}) collective-permute-start(bf16[64,3072]{1,0:T(8,128)(2,1)S(1)} %select_convert_fusion.4), channel_id=1, source_target_pairs={{0,2},{1,3},{2,0},{3,1},{4,6},{5,7},{6,4},{7,5},{8,10},{9,11},{10,... | collective-permute-start | bytes 1179656 | tf_op jit(solution)/shard_map/while/body/eval_jaxpr/ppermute | solution.py:32
  481.4 10.6 %collective-permute-start.6 = (bf16[32,3072]{1,0:T(8,128)(2,1)S(1)}, bf16[32,3072]{1,0:T(8,128)(2,1)}, u32[]{:S(2)}, u32[]{:S(2)}) collective-permute-start(bf16[32,3072]{1,0:T(8,128)(2,1)S(1)} %get-tuple-element.999), channel_id=1, source_target_pairs={{0,8},{1,9},{2,10},{3,11},{4,12},{5,13},{6,14},{7,15},{16,24},{17,... | collective-permute-start | bytes 589832 | tf_op jit(solution)/shard_map/while/body/eval_jaxpr/ppermute | solution.py:38
  487.5 7.9 %collective-permute-start.7 = (bf16[32,3072]{1,0:T(8,128)(2,1)S(1)}, bf16[32,3072]{1,0:T(8,128)(2,1)S(1)}, u32[]{:S(2)}, u32[]{:S(2)}) collective-permute-start(bf16[32,3072]{1,0:T(8,128)(2,1)S(1)} %convert_select_fusion.4), channel_id=1, source_target_pairs={{0,8},{1,9},{2,10},{3,11},{4,12},{5,13},{6,14},{7,15},{16,24},{17,... | collective-permute-start | bytes 589832 | tf_op jit(solution)/shard_map/while/body/eval_jaxpr/ppermute | solution.py:38
  501.2 11.2 %collective-permute-start.1 = (bf16[64,3072]{1,0:T(8,128)(2,1)S(1)}, bf16[64,3072]{1,0:T(8,128)(2,1)S(1)}, u32[]{:S(2)}, u32[]{:S(2)}) collective-permute-start(bf16[64,3072]{1,0:T(8,128)(2,1)S(1)} %maximum_select_fusion.9), channel_id=1, source_target_pairs={{0,2},{1,3},{2,0},{3,1},{4,6},{5,7},{6,4},{7,5},{8,10},{9,11},{10,... | collective-permute-start | bytes 1179656 | tf_op jit(solution)/shard_map/while/body/eval_jaxpr/ppermute | solution.py:32
  512.6 26.7 %collective-permute-start.2 = (bf16[128,3072]{1,0:T(8,128)(2,1)S(1)}, bf16[128,3072]{1,0:T(8,128)(2,1)}, u32[]{:S(2)}, u32[]{:S(2)}) collective-permute-start(bf16[128,3072]{1,0:T(8,128)(2,1)S(1)} %maximum_select_fusion.10), channel_id=1, source_target_pairs={{0,4},{1,5},{2,6},{3,7},{4,0},{5,1},{6,2},{7,3},{8,12},{9,13},{10,... | collective-permute-start | bytes 2359304 | tf_op jit(solution)/shard_map/while/body/eval_jaxpr/ppermute | solution.py:32
  541.7 18.2 %collective-permute-start.3 = (bf16[128,3072]{1,0:T(8,128)(2,1)S(1)}, bf16[128,3072]{1,0:T(8,128)(2,1)S(1)}, u32[]{:S(2)}, u32[]{:S(2)}) collective-permute-start(bf16[128,3072]{1,0:T(8,128)(2,1)S(1)} %broadcast_select_fusion.7), channel_id=1, source_target_pairs={{0,4},{1,5},{2,6},{3,7},{4,0},{5,1},{6,2},{7,3},{8,12},{9,13},{10,... | collective-permute-start | bytes 2359304 | tf_op jit(solution)/shard_map/while/body/eval_jaxpr/ppermute | solution.py:32
  560.3 8.9 %collective-permute-start.4 = (bf16[64,3072]{1,0:T(8,128)(2,1)S(1)}, bf16[64,3072]{1,0:T(8,128)(2,1)S(1)}, u32[]{:S(2)}, u32[]{:S(2)}) collective-permute-start(bf16[64,3072]{1,0:T(8,128)(2,1)S(1)} %select_convert_fusion.4), channel_id=1, source_target_pairs={{0,2},{1,3},{2,0},{3,1},{4,6},{5,7},{6,4},{7,5},{8,10},{9,11},{10,... | collective-permute-start | bytes 1179656 | tf_op jit(solution)/shard_map/while/body/eval_jaxpr/ppermute | solution.py:32
  571.2 35.5 %collective-permute-start.6 = (bf16[32,3072]{1,0:T(8,128)(2,1)S(1)}, bf16[32,3072]{1,0:T(8,128)(2,1)}, u32[]{:S(2)}, u32[]{:S(2)}) collective-permute-start(bf16[32,3072]{1,0:T(8,128)(2,1)S(1)} %get-tuple-element.999), channel_id=1, source_target_pairs={{0,8},{1,9},{2,10},{3,11},{4,12},{5,13},{6,14},{7,15},{16,24},{17,... | collective-permute-start | bytes 589832 | tf_op jit(solution)/shard_map/while/body/eval_jaxpr/ppermute | solution.py:38
  602.2 7.9 %collective-permute-start.7 = (bf16[32,3072]{1,0:T(8,128)(2,1)S(1)}, bf16[32,3072]{1,0:T(8,128)(2,1)S(1)}, u32[]{:S(2)}, u32[]{:S(2)}) collective-permute-start(bf16[32,3072]{1,0:T(8,128)(2,1)S(1)} %convert_select_fusion.4), channel_id=1, source_target_pairs={{0,8},{1,9},{2,10},{3,11},{4,12},{5,13},{6,14},{7,15},{16,24},{17,... | collective-permute-start | bytes 589832 | tf_op jit(solution)/shard_map/while/body/eval_jaxpr/ppermute | solution.py:38
  (41 other events, 272.2 us)
Sparse Core Ops, SparseCore 0:
  612.0 65.5 reduce-scatter.1
